TPU v7x, 256 devices: a whole 4x4x8 slice. The times are simulated.
256 devices in a mesh: fsdp: 16 (over z, core), batch: 16 (over y, x).
Axes of the slice: x: 4, y: 4, z: 8, core: 2. Of those that a mesh axis runs over, the one named last changes fastest.
Arguments:
- latents: bfloat16 [16, 16, 1024, 640], P('batch', 'fsdp'), may hold values from -6 to 6
- norm_gain: float32 [640], replicated, may hold values from 0.25 to 1.75
- second_gain: float32 [640], replicated, may hold values from 0.25 to 1.75
- spatial_w: bfloat16 [9, 640, 640], P(None, None, 'fsdp'), may hold values from -0.078125 to 0.078125
- temporal_w: bfloat16 [3, 640, 640], P(None, None, 'fsdp'), may hold values from -0.125 to 0.125
- critic_w: bfloat16 [16, 640, 640], P('batch'), may hold values from -0.25 to 0.25
- critic_head: float32 [16, 640], P('batch'), may hold values from -6 to 6
- targets: int32 [16, 32, 1], P('batch'), may hold values from 0 to 15; in each aligned block of 32 rows (0 to 31, 32 to 63, ..., all dimensions but the last counted through in order) at most 4 rows name the same one
- feasible: int32 [16, 16], P('batch', 'fsdp'), may hold values 0 or 1
Outputs:
- guided: bfloat16 [16, 16, 1024, 640], P('batch', 'fsdp')
Inputs may be any that keep to these rules, and one draw needn't show every extreme that they name: `targets`: among one candidate's 32 rows no critic group is named more than 4 times.
All inputs are finite; a program needn't handle non-finite values. No bound on the sum of `feasible` on one device may be relied on, other than what follows from the above.
Results may differ from a plain program's by a relative error of at most 0.0065.
Values may be sent and summed in bfloat16 or wider, within the bound.
No kernel may reach another device: no remote copies, remote signals or barrier semaphores. Data moves between devices by JAX's collectives and lax.ppermute only.
A program may use at most 128 MiB of HBM per device.

v0:
```python
import jax
import jax.numpy as jnp
from jax import lax
from jax.sharding import PartitionSpec as P

GROUPS = 32
IMG_ROWS = 32
IMG_COLS = 32
PIX = 1024


def rows_first(arrays, axis, dims):
    turned = [jnp.moveaxis(a, dim, 0) for a, dim in zip(arrays, dims)]
    widths = [t[0].size for t in turned]
    both = jnp.concatenate([t.reshape(-1, w) for t, w in zip(turned, widths)], axis=1)
    filled = lax.all_gather(both, axis, axis=0, tiled=True)
    tiles = jnp.split(filled, [sum(widths[:k]) for k in range(1, len(widths))], axis=1)
    return tuple(
        (
            jnp.moveaxis(b.reshape(-1, *t.shape[1:]), 0, dim)
            for b, t, dim in zip(tiles, turned, dims)
        )
    )


def with_halo(array, sides, width):
    for axis, dim in sides:
        size, length = (lax.axis_size(axis), array.shape[dim])
        up = [(i, (i + 1) % size) for i in range(size - 1)]
        down = [(j, i) for i, j in up]
        last = lax.slice_in_dim(array, length - width, length, axis=dim)
        leading = lax.slice_in_dim(array, 0, width, axis=dim)
        before = lax.ppermute(last, axis, up)
        after = lax.ppermute(leading, axis, down)
        array = jnp.concatenate([before, array, after], axis=dim)
    return array


def group_silu(values, gain):
    shape = values.shape
    width = shape[-1]
    grouped = values.astype(jnp.float32).reshape(-1, shape[-2], GROUPS, width // GROUPS)
    center = jnp.mean(grouped, axis=(1, 3), keepdims=True)
    spread = jnp.mean((grouped - center) ** 2, axis=(1, 3), keepdims=True)
    normed = ((grouped - center) * lax.rsqrt(spread + 1e-05)).reshape(shape) * gain
    return jax.nn.silu(normed).astype(jnp.bfloat16)


def per_device(
    latents, norm_gain, second_gain, spatial_w, temporal_w, critic_w, critic_head, targets, feasible
):
    cands = latents.shape[0]
    width = latents.shape[-1]
    first = group_silu(latents, norm_gain)
    padded = jnp.pad(
        first.reshape(cands, IMG_ROWS, IMG_COLS, width), ((0, 0), (1, 1), (1, 1), (0, 0))
    )
    spatial_full, temporal_full = rows_first((spatial_w, temporal_w), "fsdp", (2, 2))
    total = jnp.zeros((cands * PIX, spatial_full.shape[2]), jnp.float32)
    for offset in range(9):
        row_off, col_off = divmod(offset, 3)
        window = padded[:, row_off : row_off + IMG_ROWS, col_off : col_off + IMG_COLS].reshape(
            -1, width
        )
        total = total + jnp.dot(window, spatial_full[offset], preferred_element_type=jnp.float32)
    mixed = total
    section = (latents.astype(jnp.float32) + mixed.reshape(latents.shape)).astype(jnp.bfloat16)
    second = group_silu(section, second_gain)
    beside_all = with_halo(second, (("fsdp", 1),), 1)
    total = jnp.zeros((cands * PIX, temporal_full.shape[2]), jnp.float32)
    for tap in range(3):
        total = total + jnp.dot(
            beside_all[:, tap].reshape(-1, width),
            temporal_full[tap],
            preferred_element_type=jnp.float32,
        )
    denoised = (section.astype(jnp.float32) + total.reshape(latents.shape)).astype(jnp.bfloat16)
    groups = lax.axis_size("batch")
    capacity = max(2, 2 * IMG_ROWS // groups)
    slots = cands * capacity
    flat_targets = targets.reshape(-1)
    chosen = (flat_targets[:, None] == jnp.arange(groups, dtype=jnp.int32)[None, :]).astype(
        jnp.int32
    )
    earlier = jnp.cumsum(chosen, axis=0) - chosen
    slot_of = jnp.sum(earlier * chosen, axis=1)
    live = jnp.repeat(feasible.reshape(-1), IMG_ROWS) > 0
    position = flat_targets * slots + slot_of
    placing = (
        (jnp.arange(groups * slots, dtype=jnp.int32)[:, None] == position[None, :]) & live[None, :]
    ).astype(jnp.bfloat16)
    rows = denoised.reshape(cands * IMG_ROWS, IMG_COLS * width)
    outgoing = (
        jnp.dot(placing, rows, preferred_element_type=jnp.float32)
        .astype(jnp.bfloat16)
        .reshape(groups, slots, IMG_COLS * width)
    )
    weights = lax.all_gather(critic_w, "batch", axis=0, tiled=True)
    heads = lax.all_gather(critic_head.astype(jnp.bfloat16), "batch", axis=0, tiled=True).astype(
        jnp.float32
    )
    count = weights.shape[0]
    block = outgoing.reshape(count, -1, width)
    pre = jnp.einsum("gtc,gch->gth", block, weights, preferred_element_type=jnp.float32)
    slope = ((1.0 - jnp.tanh(pre) ** 2) * heads[:, None, :]).astype(jnp.bfloat16)
    grads = jnp.einsum("gth,gch->gtc", slope, weights, preferred_element_type=jnp.float32).astype(
        jnp.bfloat16
    )
    returned = grads.reshape(count, slots, -1)
    back = jnp.dot(
        placing.T, returned.reshape(groups * slots, -1), preferred_element_type=jnp.float32
    )
    guided = (rows.astype(jnp.float32) - back).astype(jnp.bfloat16)
    return guided.reshape(latents.shape)


def solution(mesh):
    in_specs = (
        P("batch", "fsdp", None, None),
        P(),
        P(),
        P(None, None, "fsdp"),
        P(None, None, "fsdp"),
        P("batch", None, None),
        P("batch", None),
        P("batch", None, None),
        P("batch", "fsdp"),
    )
    out_specs = P("batch", "fsdp", None, None)
    return jax.shard_map(
        per_device, mesh=mesh, in_specs=in_specs, out_specs=out_specs, check_vma=False
    )
```

profile of v0, /device:TPU:64, one launch (start us, length us, event | category | flops | bytes accessed | tf_op | source)
XLA Modules:
  0.0 205.3 jit_solution(7724707454075082725)
XLA Ops:
  6.5 1.2 copy.19
  7.7 0.9 copy.20
  12.7 5.3 %pad_slice_fusion = (bf16[1,32,32,640]{3,2,1,0:T(8,128)(2,1)}, bf16[1,32,32,640]{3,2,1,0:T(8,128)(2,1)}, bf16[1,32,32,640]{3,2,1,0:T(8,128)(2,1)}, bf16[1,32,32,...) fusion(bf16[1,32,32,640]{3,2,1,0:T(8,128)(2,1)S(1)} %bitcast.109), kind=kLoop, calls=%fused_computation.36 | loop fusion | bytes 11796480 | tf_op jit(solution)/shard_map/slice | solution.py:62
  18.0 54.8 %all-gather.4.cloned.1.call-done = bf16[640,7680]{1,0:T(8,128)(2,1)} async-done(((bf16[40,7680]{1,0:T(8,128)(2,1)}), bf16[640,7680]{1,0:T(8,128)(2,1)}) %all-gather.4.cloned.1.call-update) | async-done | bytes 9830416 | tf_op jit(solution)/shard_map/all_gather | solution.py:16
  72.7 6.6 %split.8 = bf16[640,5760]{1,0:T(8,128)(2,1)} slice(bf16[640,7680]{1,0:T(8,128)(2,1)} %all-gather.4.cloned.1.call-done), slice={[0:640], [0:5760]} | slice | bytes 14745600 | tf_op jit(solution)/shard_map/split | solution.py:17
  79.3 10.4 %copy.16 = bf16[640,5760]{0,1:T(8,128)(2,1)} copy(bf16[640,5760]{1,0:T(8,128)(2,1)} %split.8) | data formatting | bytes 14745600 | tf_op jit(solution)/shard_map/split | solution.py:17
  89.7 2.6 %fusion.35 = f32[1024,640]{1,0:T(8,128)S(1)} fusion(bf16[1,1,1024,640]{3,2,1,0:T(8,128)(2,1)S(1)} %fusion.20, bf16[9,640,640]{2,1,0:T(8,128)(2,1)} %bitcast.100), kind=kOutput, calls=%fused_computation.50 | convolution fusion | flops 838860800 | bytes 4751360 | tf_op jit(solution)/shard_map/dot_general | solution.py:65
  93.4 1.3 fusion.39
  94.7 1.3 fusion.40
  96.1 1.3 fusion.41
  97.4 1.3 fusion.42
  98.8 2.8 %fusion.43 = f32[1024,640]{1,0:T(8,128)} fusion(bf16[1024,640]{1,0:T(8,128)(2,1)S(1)} %bitcast.117, bf16[9,640,640]{2,1,0:T(8,128)(2,1)S(1)} %bitcast.105), kind=kOutput, calls=%fused_computation.67 | convolution fusion | flops 838860800 | bytes 4751360 | tf_op jit(solution)/shard_map/dot_general | solution.py:65
  101.6 2.9 %fusion.44 = f32[1024,640]{1,0:T(8,128)} fusion(bf16[1024,640]{1,0:T(8,128)(2,1)S(1)} %bitcast.116, bf16[9,640,640]{2,1,0:T(8,128)(2,1)S(1)} %bitcast.106), kind=kOutput, calls=%fused_computation.69 | convolution fusion | flops 838860800 | bytes 4751360 | tf_op jit(solution)/shard_map/dot_general | solution.py:65
  104.5 2.9 %fusion.45 = f32[1024,640]{1,0:T(8,128)} fusion(bf16[1024,640]{1,0:T(8,128)(2,1)S(1)} %bitcast.115, bf16[9,640,640]{2,1,0:T(8,128)(2,1)S(1)} %bitcast.107), kind=kOutput, calls=%fused_computation.71 | convolution fusion | flops 838860800 | bytes 4751360 | tf_op jit(solution)/shard_map/dot_general | solution.py:65
  107.4 5.1 %convert_reduce_fusion = (f32[640]{0:T(1024)S(1)}, bf16[1,1,1024,640]{3,2,1,0:T(8,128)(2,1)S(1)}) fusion(bf16[1024,640]{1,0:T(8,128)(2,1)S(1)} %bitcast.110, bf16[9,640,640]{2,1,0:T(8,128)(2,1)S(1)} %bitcast.108, f32[1024,640]{1,0:T(8,128)S(1)} %fusion.39, f32[1024,640]{1,0:T(8,128)S(1)} %fusion.40, f32[1024,640]{1,0:T(8,128)S(1)} %fusion.41, ...), kind=kOutput, calls=%fused_computation.6 | convolution fusion | flops 847379840 | bytes 25725440 | tf_op jit(solution)/shard_map/dot_general | solution.py:65
  113.7 2.1 %fusion.12 = bf16[1,1,1024,640]{3,2,1,0:T(8,128)(2,1)} fusion(bf16[1,1,1024,640]{3,2,1,0:T(8,128)(2,1)S(1)} %get-tuple-element.14, f32[640]{0:T(1024)S(1)} %copy-done.12, f32[640]{0:T(1024)S(1)} %mul.92, f32[640]{0:T(1024)S(1)} %sub.61), kind=kLoop, calls=%fused_computation.21 | loop fusion | flops 5898240 | bytes 2629120 | tf_op jit(solution)/shard_map/convert_element_type | solution.py:46
  115.8 2.1 %collective-permute-start = (bf16[1,1,1024,640]{3,2,1,0:T(8,128)(2,1)}, bf16[1,1,1024,640]{3,2,1,0:T(8,128)(2,1)}, u32[]{:S(2)}, u32[]{:S(2)}) collective-permute-start(bf16[1,1,1024,640]{3,2,1,0:T(8,128)(2,1)} %fusion.12), channel_id=1, source_target_pairs={{0,16},{16,32},{32,48},{48,64},{64,80},{80,96},{96,112},{112,128},... | collective-permute-start | bytes 3932168 | tf_op jit(solution)/shard_map/ppermute | solution.py:33
  118.0 3.4 %collective-permute-start.1 = (bf16[1,1,1024,640]{3,2,1,0:T(8,128)(2,1)}, bf16[1,1,1024,640]{3,2,1,0:T(8,128)(2,1)S(1)}, u32[]{:S(2)}, u32[]{:S(2)}) collective-permute-start(bf16[1,1,1024,640]{3,2,1,0:T(8,128)(2,1)} %fusion.12), channel_id=1, source_target_pairs={{16,0},{32,16},{48,32},{64,48},{80,64},{96,80},{112,96},{128,112},... | collective-permute-start | bytes 3932168 | tf_op jit(solution)/shard_map/ppermute | solution.py:34
  122.1 24.6 %all-gather = bf16[16,1,640]{2,1,0:T(2,128)(2,1)S(1)} all-gather(bf16[1,1,640]{2,1,0:T(2,128)(2,1)S(1)} %convert_bitcast_fusion), channel_id=1, replica_groups=mesh['fsdp'=16,'batch'=16] {'batch'}, dimensions={0}, use_global_device_ids=true | all-gather | bytes 21760 | tf_op jit(solution)/shard_map/all_gather | solution.py:99
  147.0 3.4 %split.9 = bf16[640,1920]{1,0:T(8,128)(2,1)} slice(bf16[640,7680]{1,0:T(8,128)(2,1)} %all-gather.4.cloned.1.call-done), slice={[0:640], [5760:7680]} | slice | bytes 4915200 | tf_op jit(solution)/shard_map/split | solution.py:17
  150.4 4.3 %copy.17 = bf16[640,1920]{0,1:T(8,128)(2,1)} copy(bf16[640,1920]{1,0:T(8,128)(2,1)} %split.9) | data formatting | bytes 4915200 | tf_op jit(solution)/shard_map/split | solution.py:17
  154.8 3.0 %fusion.31 = f32[1024,640]{1,0:T(8,128)S(1)} fusion(bf16[1,1,1024,640]{3,2,1,0:T(8,128)(2,1)} %fusion.12, bf16[3,640,640]{2,1,0:T(8,128)(2,1)} %bitcast.111), kind=kOutput, calls=%fused_computation.46 | convolution fusion | flops 838860800 | bytes 4751360 | tf_op jit(solution)/shard_map/dot_general | solution.py:72
  157.8 2.7 %fusion.33 = f32[1024,640]{1,0:T(8,128)S(1)} fusion(bf16[1,1,1024,640]{3,2,1,0:T(8,128)(2,1)} %collective-permute-done, bf16[3,640,640]{2,1,0:T(8,128)(2,1)S(1)} %bitcast.112), kind=kOutput, calls=%fused_computation.48 | convolution fusion | flops 838860800 | bytes 4751360 | tf_op jit(solution)/shard_map/dot_general | solution.py:72
  160.5 2.5 %fusion.22 = bf16[1,1,1024,640]{3,2,1,0:T(8,128)(2,1)} fusion(bf16[1,1,1024,640]{3,2,1,0:T(8,128)(2,1)S(1)} %get-tuple-element.14, f32[1024,640]{1,0:T(8,128)S(1)} %fusion.33, f32[1024,640]{1,0:T(8,128)S(1)} %fusion.31, bf16[1,1,1024,640]{3,2,1,0:T(8,128)(2,1)S(1)} %collective-permute-done.1, bf16[3,640,640]{2,1,0:T(8,128)(2,1)S(1)} %bitcast.113), kind=kOutput, calls=%fused_computation.31 | convolution fusion | flops 842137600 | bytes 9994240 | tf_op jit(solution)/shard_map/dot_general | solution.py:72
  163.1 1.7 reshape.224
  164.8 2.3 %convolution_convert_fusion = bf16[64,20480]{1,0:T(8,128)(2,1)} fusion(bf16[32,20480]{1,0:T(8,128)(2,1)S(1)} %reshape.224, s32[32]{0:T(128)S(1)} %multiply_add_fusion, pred[]{:T(512)} %bitcast.36), kind=kOutput, calls=%fused_computation | convolution fusion | flops 85200896 | bytes 3932289 | tf_op jit(solution)/shard_map/dot_general | solution.py:94
  167.1 4.6 %reshape_reshape.6 = bf16[16,128,640]{2,1,0:T(8,128)(2,1)} reshape(bf16[64,20480]{1,0:T(8,128)(2,1)} %convolution_convert_fusion) | data formatting | bytes 5242880 | tf_op jit(solution)/shard_map/reshape;reshape | solution.py:103
  171.6 1.9 all-gather.6.cloned.1.call-done
  173.5 16.6 %fusion.26 = bf16[16,128,640]{2,1,0:T(8,128)(2,1)} fusion(bf16[16,640,640]{2,1,0:T(8,128)(2,1)} %all-gather.6.cloned.1.call-done, f32[16,640]{1,0:T(8,128)S(1)} %bitcast.125, bf16[16,128,640]{2,1,0:T(8,128)(2,1)} %reshape_reshape.6), kind=kOutput, calls=%fused_computation.35 | convolution fusion | flops 3361996800 | bytes 18391040 | tf_op jit(solution)/shard_map/gth,gch->gtc/dot_general | solution.py:106
  190.2 4.5 %reshape_reshape.7 = bf16[64,20480]{1,0:T(8,128)(2,1)} reshape(bf16[16,128,640]{2,1,0:T(8,128)(2,1)} %fusion.26) | data formatting | bytes 5242880 | tf_op jit(solution)/shard_map/reshape;reshape | solution.py:111
  194.7 2.3 %fusion = bf16[32,20480]{1,0:T(8,128)(2,1)S(1)} fusion(bf16[64,20480]{1,0:T(8,128)(2,1)} %reshape_reshape.7, bf16[32,20480]{1,0:T(8,128)(2,1)S(1)} %reshape.224, s32[32]{0:T(128)S(1)} %multiply_add_fusion, pred[]{:T(512)} %bitcast.36), kind=kOutput, calls=%fused_computation.2 | convolution fusion | flops 85856256 | bytes 5243009 | tf_op jit(solution)/shard_map/dot_general | solution.py:110
  197.0 1.5 reshape.226
  (67 shorter events, 6.7 us)
Async XLA Ops:
  6.5 3.8 %copy-start = (bf16[1,1,1024,640]{3,2,1,0:T(8,128)(2,1)S(1)}, bf16[1,1,1024,640]{3,2,1,0:T(8,128)(2,1)}, u32[]{:S(2)}) copy-start(bf16[1,1,1024,640]{3,2,1,0:T(8,128)(2,1)} %param.9) | copy-start | bytes 3932164
  6.5 66.2 %all-gather.4.cloned.1.call-start = ((), (), s32[]{:S(2)}) async-start(), calls=%async_computation | async-start | bytes 10444800 | tf_op jit(solution)/shard_map/all_gather | solution.py:16
  8.6 3.2 %copy-start.11 = (f32[640]{0:T(1024)S(1)}, f32[640]{0:T(1024)}, u32[]{:S(2)}) copy-start(f32[640]{0:T(1024)} %param.10) | copy-start | bytes 7684
  9.6 164.0 %all-gather.6.cloned.1.call-start = ((), (), s32[]{:S(2)}) async-start(), calls=%async_computation.1 | async-start | bytes 13926400 | tf_op jit(solution)/shard_map/all_gather | solution.py:98
  89.7 3.4 %copy-start.1 = (bf16[640,5760]{0,1:T(8,128)(2,1)S(1)}, bf16[640,5760]{0,1:T(8,128)(2,1)}, u32[]{:S(2)}) copy-start(bf16[640,5760]{0,1:T(8,128)(2,1)} %copy.16) | copy-start | bytes 22118404
  89.7 3.7 %copy-start.10 = (bf16[1,32,32,640]{3,2,1,0:T(8,128)(2,1)S(1)}, bf16[1,32,32,640]{3,2,1,0:T(8,128)(2,1)}, u32[]{:S(2)}) copy-start(bf16[1,32,32,640]{3,2,1,0:T(8,128)(2,1)} %get-tuple-element.11) | copy-start | bytes 3932164
  93.4 1.3 copy-start.9
  94.7 1.3 copy-start.8
  96.1 1.3 copy-start.7
  97.4 1.4 copy-start.6
  98.8 2.8 %copy-start.5 = (bf16[1,32,32,640]{3,2,1,0:T(8,128)(2,1)S(1)}, bf16[1,32,32,640]{3,2,1,0:T(8,128)(2,1)}, u32[]{:S(2)}) copy-start(bf16[1,32,32,640]{3,2,1,0:T(8,128)(2,1)} %get-tuple-element.6) | copy-start | bytes 3932164
  101.6 2.9 %copy-start.4 = (bf16[1,32,32,640]{3,2,1,0:T(8,128)(2,1)S(1)}, bf16[1,32,32,640]{3,2,1,0:T(8,128)(2,1)}, u32[]{:S(2)}) copy-start(bf16[1,32,32,640]{3,2,1,0:T(8,128)(2,1)} %get-tuple-element.12) | copy-start | bytes 3932164
  104.5 2.9 %copy-start.2 = (bf16[1,32,32,640]{3,2,1,0:T(8,128)(2,1)S(1)}, bf16[1,32,32,640]{3,2,1,0:T(8,128)(2,1)}, u32[]{:S(2)}) copy-start(bf16[1,32,32,640]{3,2,1,0:T(8,128)(2,1)} %get-tuple-element.5) | copy-start | bytes 3932164
  107.4 6.3 %copy-start.12 = (f32[640]{0:T(1024)S(1)}, f32[640]{0:T(1024)}, u32[]{:S(2)}) copy-start(f32[640]{0:T(1024)} %param.11) | copy-start | bytes 7684
  112.5 8.9 %copy-start.13 = (f32[1,640]{1,0:T(1,128)S(1)}, f32[1,640]{1,0:T(1,128)}, u32[]{:S(2)}) copy-start(f32[1,640]{1,0:T(1,128)} %param.15) | copy-start | bytes 7684
  112.5 34.2 %copy-start.14 = (s32[1,32,1]{1,2,0:T(1,128)S(1)}, s32[1,32,1]{1,2,0:T(1,128)}, u32[]{:S(2)}) copy-start(s32[1,32,1]{1,2,0:T(1,128)} %param.16) | copy-start | bytes 388
  115.8 41.9 %collective-permute-start = (bf16[1,1,1024,640]{3,2,1,0:T(8,128)(2,1)}, bf16[1,1,1024,640]{3,2,1,0:T(8,128)(2,1)}, u32[]{:S(2)}, u32[]{:S(2)}) collective-permute-start(bf16[1,1,1024,640]{3,2,1,0:T(8,128)(2,1)} %fusion.12), channel_id=1, source_target_pairs={{0,16},{16,32},{32,48},{48,64},{64,80},{80,96},{96,112},{112,128},... | collective-permute-start | bytes 3932168 | tf_op jit(solution)/shard_map/ppermute | solution.py:33
  118.0 42.5 %collective-permute-start.1 = (bf16[1,1,1024,640]{3,2,1,0:T(8,128)(2,1)}, bf16[1,1,1024,640]{3,2,1,0:T(8,128)(2,1)S(1)}, u32[]{:S(2)}, u32[]{:S(2)}) collective-permute-start(bf16[1,1,1024,640]{3,2,1,0:T(8,128)(2,1)} %fusion.12), channel_id=1, source_target_pairs={{16,0},{32,16},{48,32},{64,48},{80,64},{96,80},{112,96},{128,112},... | collective-permute-start | bytes 3932168 | tf_op jit(solution)/shard_map/ppermute | solution.py:34
  154.8 3.0 %copy-start.3 = (bf16[640,1920]{0,1:T(8,128)(2,1)S(1)}, bf16[640,1920]{0,1:T(8,128)(2,1)}, u32[]{:S(2)}) copy-start(bf16[640,1920]{0,1:T(8,128)(2,1)} %copy.17) | copy-start | bytes 7372804
Sparse Core Ops, SparseCore 0:
  9.7 63.0 all-gather.3
  75.2 98.3 all-gather.5
where the time goes:
time: 208 us; the launch traced here: 205 us
  waiting for transfers between devices  57.4 us (28%)
  matrix products  51 us (25%)
  local copies, waits for them, and re-layouts  46.7 us (22%)
  blocking collectives  24.6 us (12%)
  between operations  14.4 us (7%)
  other arithmetic  5.68 us (3%)
  starting transfers between devices  5.6 us (3%)
    all_gather x1, waiting for transfers between devices, rows_first(): filled = lax.all_gather(both, axis, axis=0, tiled=True)  54.8 us
    split x4, local copies, waits for them, and re-layouts, rows_first(): jnp.split(filled, [sum(widths[:k]) for k in range(1, len(widths))], axis=1)  24.7 us
    all_gather x1, blocking collectives, per_device(): lax.all_gather(critic_head.astype(jnp.bfloat16), 'batch', axis=0, tiled=T...  24.6 us
    dot_general x9, matrix products, per_device(): jnp.dot(window, spatial_full[offset], preferred_element_type=jnp.float32)  21.5 us
    dot_general x1, matrix products, per_device(): jnp.einsum('gth,gch->gtc', slope, weights, preferred_element_type=jnp.flo...  16.6 us
    dot_general x3, matrix products, per_device(): jnp.dot(beside_all[:, tap].reshape(-1, width), temporal_full[tap], prefer...  8.22 us
    slice x1, local copies, waits for them, and re-layouts, per_device(): padded[:, row_off:row_off + IMG_ROWS, col_off:col_off + IMG_COLS]  5.3 us
    another operation x1, local copies, waits for them, and re-layouts, per_device(): block = outgoing.reshape(count, -1, width)  4.55 us
  transfers between devices with their start and end apart: 4, of which 2 were waited for; matrix products, arithmetic and copies ran while one was open for 36% of the time, Pallas kernels for 0%

commit v1 on v0

--- a/solution.py
+++ b/solution.py
@@ -7,20 +7,7 @@
 IMG_ROWS = 32
 IMG_COLS = 32
 PIX = 1024
-
-
-def rows_first(arrays, axis, dims):
-    turned = [jnp.moveaxis(a, dim, 0) for a, dim in zip(arrays, dims)]
-    widths = [t[0].size for t in turned]
-    both = jnp.concatenate([t.reshape(-1, w) for t, w in zip(turned, widths)], axis=1)
-    filled = lax.all_gather(both, axis, axis=0, tiled=True)
-    tiles = jnp.split(filled, [sum(widths[:k]) for k in range(1, len(widths))], axis=1)
-    return tuple(
-        (
-            jnp.moveaxis(b.reshape(-1, *t.shape[1:]), 0, dim)
-            for b, t, dim in zip(tiles, turned, dims)
-        )
-    )
+CAP = 4
 
 
 def with_halo(array, sides, width):
@@ -55,7 +42,8 @@
     padded = jnp.pad(
         first.reshape(cands, IMG_ROWS, IMG_COLS, width), ((0, 0), (1, 1), (1, 1), (0, 0))
     )
-    spatial_full, temporal_full = rows_first((spatial_w, temporal_w), "fsdp", (2, 2))
+    spatial_full = lax.all_gather(spatial_w, "fsdp", axis=2, tiled=True)
+    temporal_full = lax.all_gather(temporal_w, "fsdp", axis=2, tiled=True)
     total = jnp.zeros((cands * PIX, spatial_full.shape[2]), jnp.float32)
     for offset in range(9):
         row_off, col_off = divmod(offset, 3)
@@ -63,8 +51,7 @@
             -1, width
         )
         total = total + jnp.dot(window, spatial_full[offset], preferred_element_type=jnp.float32)
-    mixed = total
-    section = (latents.astype(jnp.float32) + mixed.reshape(latents.shape)).astype(jnp.bfloat16)
+    section = (latents.astype(jnp.float32) + total.reshape(latents.shape)).astype(jnp.bfloat16)
     second = group_silu(section, second_gain)
     beside_all = with_halo(second, (("fsdp", 1),), 1)
     total = jnp.zeros((cands * PIX, temporal_full.shape[2]), jnp.float32)
@@ -75,9 +62,9 @@
             preferred_element_type=jnp.float32,
         )
     denoised = (section.astype(jnp.float32) + total.reshape(latents.shape)).astype(jnp.bfloat16)
+
     groups = lax.axis_size("batch")
-    capacity = max(2, 2 * IMG_ROWS // groups)
-    slots = cands * capacity
+    slots = cands * CAP
     flat_targets = targets.reshape(-1)
     chosen = (flat_targets[:, None] == jnp.arange(groups, dtype=jnp.int32)[None, :]).astype(
         jnp.int32
@@ -93,20 +80,18 @@
     outgoing = (
         jnp.dot(placing, rows, preferred_element_type=jnp.float32)
         .astype(jnp.bfloat16)
-        .reshape(groups, slots, IMG_COLS * width)
+        .reshape(groups, slots * IMG_COLS, width)
     )
-    weights = lax.all_gather(critic_w, "batch", axis=0, tiled=True)
-    heads = lax.all_gather(critic_head.astype(jnp.bfloat16), "batch", axis=0, tiled=True).astype(
-        jnp.float32
+    arrived = lax.all_to_all(outgoing, "batch", 0, 0, tiled=True)
+    own_w = critic_w[0]
+    pre = jnp.dot(arrived.reshape(-1, width), own_w, preferred_element_type=jnp.float32)
+    slope = ((1.0 - jnp.tanh(pre) ** 2) * critic_head[0][None, :]).astype(jnp.bfloat16)
+    grads = lax.dot_general(
+        slope, own_w, (((1,), (1,)), ((), ())), preferred_element_type=jnp.float32
+    ).astype(jnp.bfloat16)
+    returned = lax.all_to_all(
+        grads.reshape(groups, slots * IMG_COLS, width), "batch", 0, 0, tiled=True
     )
-    count = weights.shape[0]
-    block = outgoing.reshape(count, -1, width)
-    pre = jnp.einsum("gtc,gch->gth", block, weights, preferred_element_type=jnp.float32)
-    slope = ((1.0 - jnp.tanh(pre) ** 2) * heads[:, None, :]).astype(jnp.bfloat16)
-    grads = jnp.einsum("gth,gch->gtc", slope, weights, preferred_element_type=jnp.float32).astype(
-        jnp.bfloat16
-    )
-    returned = grads.reshape(count, slots, -1)
     back = jnp.dot(
         placing.T, returned.reshape(groups * slots, -1), preferred_element_type=jnp.float32
     )

time: 208 us -> 235 us (1.13)
  waiting for transfers between devices: 57.4 us -> 97.8 us
  local copies, waits for them, and re-layouts: 46.7 us -> 18.7 us
  blocking collectives: 24.6 us -> 38.2 us
  starting transfers between devices: 5.6 us -> 12.6 us
  matrix products: 51 us -> 46.2 us
    all_to_all x0 -> x1, waiting for transfers between devices: none -> 41.5 us  [per_device(): arrived = lax.all_to_all(outgoing, 'batch', 0, 0, tiled=True)]
    all_to_all x0 -> x1, blocking collectives: none -> 38.2 us  [per_device(): lax.all_to_all(grads.reshape(groups, slots * IMG_COLS, width), 'batch', 0...]
    split x4 -> x0, local copies, waits for them, and re-layouts: 24.7 us -> none  [rows_first(): jnp.split(filled, [sum(widths[:k]) for k in range(1, len(widths))], axis=1)]
    all_gather x1 -> x0, blocking collectives: 24.6 us -> none  [per_device(): lax.all_gather(critic_head.astype(jnp.bfloat16), 'batch', axis=0, tiled=T...]
    dot_general x1, matrix products: 16.6 us -> 7.38 us  [per_device(): lax.dot_general(slope, own_w, (((1,), (1,)), ((), ())), preferred_element...]
    another operation x2 -> x0, local copies, waits for them, and re-layouts: 9.05 us -> none  [the longest x1 4.55 us: per_device(): block = outgoing.reshape(count, -1, width)]
    all_gather x2, waiting for transfers between devices: 56.7 us -> 48.2 us  [the longest x1 44.3 us: per_device(): spatial_full = lax.all_gather(spatial_w, 'fsdp', axis=2, tiled=True)]
    all_to_all x0 -> x1, starting transfers between devices: none -> 6.98 us  [per_device(): arrived = lax.all_to_all(outgoing, 'batch', 0, 0, tiled=True)]
  transfers between devices with their start and end apart: 4 -> 5, of which waited for: 2 -> 4; matrix products, arithmetic and copies ran while one was open for 36% -> 19% of each run, Pallas kernels for 0% -> 0%
where the time goes in v1:
time: 235 us; the launch traced here: 234 us
  waiting for transfers between devices  97.8 us (42%)
  matrix products  46.2 us (20%)
  blocking collectives  38.2 us (16%)
  local copies, waits for them, and re-layouts  18.7 us (8%)
  between operations  14.4 us (6%)
  starting transfers between devices  12.6 us (5%)
  other arithmetic  6.12 us (3%)
    all_gather x1, waiting for transfers between devices, per_device(): spatial_full = lax.all_gather(spatial_w, 'fsdp', axis=2, tiled=True)  44.3 us
    all_to_all x1, waiting for transfers between devices, per_device(): arrived = lax.all_to_all(outgoing, 'batch', 0, 0, tiled=True)  41.5 us
    all_to_all x1, blocking collectives, per_device(): lax.all_to_all(grads.reshape(groups, slots * IMG_COLS, width), 'batch', 0...  38.2 us
    dot_general x9, matrix products, per_device(): jnp.dot(window, spatial_full[offset], preferred_element_type=jnp.float32)  25.9 us
    dot_general x3, matrix products, per_device(): jnp.dot(beside_all[:, tap].reshape(-1, width), temporal_full[tap], prefer...  8.22 us
    dot_general x1, matrix products, per_device(): lax.dot_general(slope, own_w, (((1,), (1,)), ((), ())), preferred_element...  7.38 us
    all_to_all x1, starting transfers between devices, per_device(): arrived = lax.all_to_all(outgoing, 'batch', 0, 0, tiled=True)  6.98 us
    ppermute x1, waiting for transfers between devices, with_halo(): before = lax.ppermute(last, axis, up)  6.67 us
  transfers between devices with their start and end apart: 5, of which 4 were waited for; matrix products, arithmetic and copies ran while one was open for 19% of the time, Pallas kernels for 0%

profile of v1, /device:TPU:64, one launch (start us, length us, event | category | flops | bytes accessed | tf_op | source)
XLA Modules:
  0.0 234.0 jit_solution(8784276038473002081)
XLA Ops:
  6.5 0.7 all-gather.3.cloned.1.call-update
  8.0 1.6 convert_reduce_fusion.1
  10.8 0.8 fusion.20
  11.7 5.3 %pad_slice_fusion = (bf16[1,32,32,640]{3,2,1,0:T(8,128)(2,1)}, bf16[1,32,32,640]{3,2,1,0:T(8,128)(2,1)}, bf16[1,32,32,640]{3,2,1,0:T(8,128)(2,1)}, bf16[1,32,32,...) fusion(bf16[1,32,32,640]{3,2,1,0:T(8,128)(2,1)S(1)} %bitcast.87), kind=kLoop, calls=%fused_computation.33 | loop fusion | bytes 11796480 | tf_op jit(solution)/shard_map/slice | solution.py:50
  17.0 44.3 %all-gather.3.cloned.1.call-done = bf16[9,640,640]{1,2,0:T(8,128)(2,1)} async-done(((bf16[9,640,40]{1,2,0:T(8,128)(2,1)}), bf16[9,640,640]{1,2,0:T(8,128)(2,1)}) %all-gather.3.cloned.1.call-update) | async-done | bytes 7372816 | tf_op jit(solution)/shard_map/all_gather | solution.py:45
  61.3 2.6 %fusion.31 = f32[1024,640]{1,0:T(8,128)S(1)} fusion(bf16[1,1,1024,640]{3,2,1,0:T(8,128)(2,1)S(1)} %fusion.20, bf16[9,640,640]{1,2,0:T(8,128)(2,1)} %all-gather.3.cloned.1.call-done), kind=kOutput, calls=%fused_computation.47 | convolution fusion | flops 838860800 | bytes 4751360 | tf_op jit(solution)/shard_map/dot_general | solution.py:53
  63.9 2.6 %fusion.33 = f32[1024,640]{1,0:T(8,128)S(1)} fusion(bf16[1024,640]{1,0:T(8,128)(2,1)S(1)} %bitcast.96, bf16[9,640,640]{1,2,0:T(8,128)(2,1)} %all-gather.3.cloned.1.call-done), kind=kOutput, calls=%fused_computation.54 | convolution fusion | flops 838860800 | bytes 4751360 | tf_op jit(solution)/shard_map/dot_general | solution.py:53
  66.5 2.6 %fusion.34 = f32[1024,640]{1,0:T(8,128)S(1)} fusion(bf16[1024,640]{1,0:T(8,128)(2,1)S(1)} %bitcast.95, bf16[9,640,640]{1,2,0:T(8,128)(2,1)} %all-gather.3.cloned.1.call-done), kind=kOutput, calls=%fused_computation.56 | convolution fusion | flops 838860800 | bytes 4751360 | tf_op jit(solution)/shard_map/dot_general | solution.py:53
  69.1 2.6 %fusion.35 = f32[1024,640]{1,0:T(8,128)S(1)} fusion(bf16[1024,640]{1,0:T(8,128)(2,1)S(1)} %bitcast.94, bf16[9,640,640]{1,2,0:T(8,128)(2,1)} %all-gather.3.cloned.1.call-done), kind=kOutput, calls=%fused_computation.58 | convolution fusion | flops 838860800 | bytes 4751360 | tf_op jit(solution)/shard_map/dot_general | solution.py:53
  71.7 2.6 %fusion.36 = f32[1024,640]{1,0:T(8,128)S(1)} fusion(bf16[1024,640]{1,0:T(8,128)(2,1)S(1)} %bitcast.93, bf16[9,640,640]{1,2,0:T(8,128)(2,1)} %all-gather.3.cloned.1.call-done), kind=kOutput, calls=%fused_computation.61 | convolution fusion | flops 838860800 | bytes 4751360 | tf_op jit(solution)/shard_map/dot_general | solution.py:53
  74.3 2.6 %fusion.37 = f32[1024,640]{1,0:T(8,128)S(1)} fusion(bf16[1024,640]{1,0:T(8,128)(2,1)S(1)} %bitcast.92, bf16[9,640,640]{1,2,0:T(8,128)(2,1)} %all-gather.3.cloned.1.call-done), kind=kOutput, calls=%fused_computation.63 | convolution fusion | flops 838860800 | bytes 4751360 | tf_op jit(solution)/shard_map/dot_general | solution.py:53
  76.9 2.6 %fusion.38 = f32[1024,640]{1,0:T(8,128)S(1)} fusion(bf16[1024,640]{1,0:T(8,128)(2,1)S(1)} %bitcast.91, bf16[9,640,640]{1,2,0:T(8,128)(2,1)} %all-gather.3.cloned.1.call-done), kind=kOutput, calls=%fused_computation.65 | convolution fusion | flops 838860800 | bytes 4751360 | tf_op jit(solution)/shard_map/dot_general | solution.py:53
  79.5 4.1 %fusion.39 = f32[1024,640]{1,0:T(8,128)} fusion(bf16[1024,640]{1,0:T(8,128)(2,1)S(1)} %bitcast.90, bf16[9,640,640]{1,2,0:T(8,128)(2,1)} %all-gather.3.cloned.1.call-done), kind=kOutput, calls=%fused_computation.67 | convolution fusion | flops 838860800 | bytes 4751360 | tf_op jit(solution)/shard_map/dot_general | solution.py:53
  83.7 3.8 %convert_reduce_fusion = (f32[640]{0:T(1024)S(1)}, bf16[1,1,1024,640]{3,2,1,0:T(8,128)(2,1)S(1)}) fusion(bf16[1024,640]{1,0:T(8,128)(2,1)S(1)} %bitcast.88, bf16[9,640,640]{1,2,0:T(8,128)(2,1)} %all-gather.3.cloned.1.call-done, f32[1024,640]{1,0:T(8,128)S(1)} %fusion.33, f32[1024,640]{1,0:T(8,128)S(1)} %fusion.34, f32[1024,640]{1,0:T(8,128)S(1)} %fusion.35, ...), kind=kOutput, calls=%fused_computation.6 | convolution fusion | flops 847379840 | bytes 25725440 | tf_op jit(solution)/shard_map/dot_general | solution.py:53
  88.7 2.1 fusion.12
  90.8 2.2 collective-permute-start
  93.0 3.4 %collective-permute-start.1 = (bf16[1,1,1024,640]{3,2,1,0:T(8,128)(2,1)}, bf16[1,1,1024,640]{3,2,1,0:T(8,128)(2,1)S(1)}, u32[]{:S(2)}, u32[]{:S(2)}) collective-permute-start(bf16[1,1,1024,640]{3,2,1,0:T(8,128)(2,1)} %fusion.12), channel_id=1, source_target_pairs={{16,0},{32,16},{48,32},{64,48},{80,64},{96,80},{112,96},{128,112},... | collective-permute-start | bytes 3932168 | tf_op jit(solution)/shard_map/ppermute | solution.py:21
  97.4 3.9 %all-gather.5.cloned.1.call-done = bf16[3,640,640]{1,2,0:T(8,128)(2,1)} async-done(((bf16[3,640,40]{1,2,0:T(8,128)(2,1)}), bf16[3,640,640]{1,2,0:T(8,128)(2,1)}) %all-gather.5.cloned.1.call-update) | async-done | bytes 2457616 | tf_op jit(solution)/shard_map/all_gather | solution.py:46
  101.3 3.0 %fusion.27 = f32[1024,640]{1,0:T(8,128)S(1)} fusion(bf16[1,1,1024,640]{3,2,1,0:T(8,128)(2,1)} %fusion.12, bf16[3,640,640]{1,2,0:T(8,128)(2,1)} %all-gather.5.cloned.1.call-done), kind=kOutput, calls=%fused_computation.43 | convolution fusion | flops 838860800 | bytes 4751360 | tf_op jit(solution)/shard_map/dot_general | solution.py:59
  104.3 6.7 %collective-permute-done = bf16[1,1,1024,640]{3,2,1,0:T(8,128)(2,1)} collective-permute-done((bf16[1,1,1024,640]{3,2,1,0:T(8,128)(2,1)}, bf16[1,1,1024,640]{3,2,1,0:T(8,128)(2,1)}, u32[]{:S(2)}, u32[]{:S(2)}) %collective-permute-start) | collective-permute-done | bytes 1310752 | tf_op jit(solution)/shard_map/ppermute | solution.py:20
  111.0 2.7 %fusion.29 = f32[1024,640]{1,0:T(8,128)S(1)} fusion(bf16[1,1,1024,640]{3,2,1,0:T(8,128)(2,1)} %collective-permute-done, bf16[3,640,640]{1,2,0:T(8,128)(2,1)S(1)} %copy-done.10), kind=kOutput, calls=%fused_computation.45 | convolution fusion | flops 838860800 | bytes 4751360 | tf_op jit(solution)/shard_map/dot_general | solution.py:59
  113.6 2.6 %fusion.22 = bf16[1,1,1024,640]{3,2,1,0:T(8,128)(2,1)} fusion(bf16[1,1,1024,640]{3,2,1,0:T(8,128)(2,1)S(1)} %get-tuple-element.14, f32[1024,640]{1,0:T(8,128)S(1)} %fusion.29, f32[1024,640]{1,0:T(8,128)S(1)} %fusion.27, bf16[1,1,1024,640]{3,2,1,0:T(8,128)(2,1)S(1)} %collective-permute-done.1, bf16[3,640,640]{1,2,0:T(8,128)(2,1)S(1)} %copy-done.10), kind=kOutput, calls=%fused_computation.32 | convolution fusion | flops 842137600 | bytes 9994240 | tf_op jit(solution)/shard_map/dot_general | solution.py:59
  116.2 1.7 reshape.219
  117.9 2.3 convolution_convert_fusion
  120.2 4.5 %reshape.221 = bf16[16,128,640]{2,1,0:T(8,128)(2,1)} reshape(bf16[64,20480]{1,0:T(8,128)(2,1)} %convolution_convert_fusion) | data formatting | bytes 5242880 | tf_op jit(solution)/shard_map/reshape | solution.py:83
  124.8 7.0 %all-to-all-start = ((bf16[16,128,640]{2,1,0:T(8,128)(2,1)}), bf16[16,128,640]{2,1,0:T(8,128)(2,1)}, u32[]{:S(2)}, u32[]{:S(2)}) async-start(bf16[16,128,640]{2,1,0:T(8,128)(2,1)} %reshape.221), calls=%async_computation | async-start | bytes 5242880 | tf_op jit(solution)/shard_map/all_to_all | solution.py:85
  131.8 41.5 %all-to-all-done = bf16[16,128,640]{2,1,0:T(8,128)(2,1)} async-done(((bf16[16,128,640]{2,1,0:T(8,128)(2,1)}), bf16[16,128,640]{2,1,0:T(8,128)(2,1)}, u32[]{:S(2)}, u32[]{:S(2)}) %all-to-all-start) | async-done | bytes 2621472 | tf_op jit(solution)/shard_map/all_to_all | solution.py:85
  173.3 7.4 %convolution_convert_fusion.1 = bf16[2048,640]{1,0:T(8,128)(2,1)} fusion(bf16[2048,640]{1,0:T(8,128)(2,1)} %bitcast.29, f32[640]{0:T(1024)S(1)} %reduce.14, bf16[1,640,640]{2,1,0:T(8,128)(2,1)S(1)} %copy-done), kind=kOutput, calls=%fused_computation.10 | convolution fusion | flops 3361996800 | bytes 6064640 | tf_op jit(solution)/shard_map/dot_general | solution.py:89
  180.6 38.2 %all_to_all.10 = bf16[16,128,640]{2,1,0:T(8,128)(2,1)} all-to-all(bf16[16,128,640]{2,1,0:T(8,128)(2,1)} %bitcast.89), channel_id=1, replica_groups=mesh['fsdp'=16,'batch'=16] {'batch'}, dimensions={0} | all-to-all | bytes 5242880 | tf_op jit(solution)/shard_map/all_to_all | solution.py:92
  218.9 4.5 %reshape.224 = bf16[64,20480]{1,0:T(8,128)(2,1)} reshape(bf16[16,128,640]{2,1,0:T(8,128)(2,1)} %all_to_all.10) | data formatting | bytes 5242880 | tf_op jit(solution)/shard_map/reshape | solution.py:96
  223.4 2.3 fusion
  225.7 1.5 reshape.225
  (61 shorter events, 3.5 us)
Async XLA Ops:
  6.5 166.7 %copy-start = (bf16[1,640,640]{2,1,0:T(8,128)(2,1)S(1)}, bf16[1,640,640]{2,1,0:T(8,128)(2,1)}, u32[]{:S(2)}) copy-start(bf16[1,640,640]{2,1,0:T(8,128)(2,1)} %param.14) | copy-start | bytes 2457604
  6.5 3.5 %copy-start.1 = (bf16[1,1,1024,640]{3,2,1,0:T(8,128)(2,1)S(1)}, bf16[1,1,1024,640]{3,2,1,0:T(8,128)(2,1)}, u32[]{:S(2)}) copy-start(bf16[1,1,1024,640]{3,2,1,0:T(8,128)(2,1)} %param.9) | copy-start | bytes 3932164
  6.5 4.3 %copy-start.11 = (f32[640]{0:T(1024)S(1)}, f32[640]{0:T(1024)}, u32[]{:S(2)}) copy-start(f32[640]{0:T(1024)} %param.10) | copy-start | bytes 7684
  6.5 54.8 %all-gather.3.cloned.1.call-start = ((), (), s32[]{:S(2)}) async-start(), calls=%async_computation.2 | async-start | bytes 7833600 | tf_op jit(solution)/shard_map/all_gather | solution.py:45
  7.3 94.0 %all-gather.5.cloned.1.call-start = ((), (), s32[]{:S(2)}) async-start(), calls=%async_computation.3 | async-start | bytes 2611200 | tf_op jit(solution)/shard_map/all_gather | solution.py:46
  61.3 2.6 %copy-start.9 = (bf16[1,32,32,640]{3,2,1,0:T(8,128)(2,1)S(1)}, bf16[1,32,32,640]{3,2,1,0:T(8,128)(2,1)}, u32[]{:S(2)}) copy-start(bf16[1,32,32,640]{3,2,1,0:T(8,128)(2,1)} %get-tuple-element.11) | copy-start | bytes 3932164
  63.9 2.6 %copy-start.8 = (bf16[1,32,32,640]{3,2,1,0:T(8,128)(2,1)S(1)}, bf16[1,32,32,640]{3,2,1,0:T(8,128)(2,1)}, u32[]{:S(2)}) copy-start(bf16[1,32,32,640]{3,2,1,0:T(8,128)(2,1)} %get-tuple-element.10) | copy-start | bytes 3932164
  66.5 2.6 %copy-start.7 = (bf16[1,32,32,640]{3,2,1,0:T(8,128)(2,1)S(1)}, bf16[1,32,32,640]{3,2,1,0:T(8,128)(2,1)}, u32[]{:S(2)}) copy-start(bf16[1,32,32,640]{3,2,1,0:T(8,128)(2,1)} %get-tuple-element.9) | copy-start | bytes 3932164
  69.1 2.6 %copy-start.6 = (bf16[1,32,32,640]{3,2,1,0:T(8,128)(2,1)S(1)}, bf16[1,32,32,640]{3,2,1,0:T(8,128)(2,1)}, u32[]{:S(2)}) copy-start(bf16[1,32,32,640]{3,2,1,0:T(8,128)(2,1)} %get-tuple-element.8) | copy-start | bytes 3932164
  71.7 2.6 %copy-start.5 = (bf16[1,32,32,640]{3,2,1,0:T(8,128)(2,1)S(1)}, bf16[1,32,32,640]{3,2,1,0:T(8,128)(2,1)}, u32[]{:S(2)}) copy-start(bf16[1,32,32,640]{3,2,1,0:T(8,128)(2,1)} %get-tuple-element.7) | copy-start | bytes 3932164
  74.3 2.6 %copy-start.4 = (bf16[1,32,32,640]{3,2,1,0:T(8,128)(2,1)S(1)}, bf16[1,32,32,640]{3,2,1,0:T(8,128)(2,1)}, u32[]{:S(2)}) copy-start(bf16[1,32,32,640]{3,2,1,0:T(8,128)(2,1)} %get-tuple-element.6) | copy-start | bytes 3932164
  76.9 2.7 %copy-start.3 = (bf16[1,32,32,640]{3,2,1,0:T(8,128)(2,1)S(1)}, bf16[1,32,32,640]{3,2,1,0:T(8,128)(2,1)}, u32[]{:S(2)}) copy-start(bf16[1,32,32,640]{3,2,1,0:T(8,128)(2,1)} %get-tuple-element.12) | copy-start | bytes 3932164
  79.5 4.2 %copy-start.2 = (bf16[1,32,32,640]{3,2,1,0:T(8,128)(2,1)S(1)}, bf16[1,32,32,640]{3,2,1,0:T(8,128)(2,1)}, u32[]{:S(2)}) copy-start(bf16[1,32,32,640]{3,2,1,0:T(8,128)(2,1)} %get-tuple-element.5) | copy-start | bytes 3932164
  83.7 5.0 %copy-start.12 = (f32[640]{0:T(1024)S(1)}, f32[640]{0:T(1024)}, u32[]{:S(2)}) copy-start(f32[640]{0:T(1024)} %param.11) | copy-start | bytes 7684
  87.4 9.6 %copy-start.14 = (s32[1,32,1]{1,2,0:T(1,128)S(1)}, s32[1,32,1]{1,2,0:T(1,128)}, u32[]{:S(2)}) copy-start(s32[1,32,1]{1,2,0:T(1,128)} %param.16) | copy-start | bytes 388
  90.8 20.1 %collective-permute-start = (bf16[1,1,1024,640]{3,2,1,0:T(8,128)(2,1)}, bf16[1,1,1024,640]{3,2,1,0:T(8,128)(2,1)}, u32[]{:S(2)}, u32[]{:S(2)}) collective-permute-start(bf16[1,1,1024,640]{3,2,1,0:T(8,128)(2,1)} %fusion.12), channel_id=1, source_target_pairs={{0,16},{16,32},{32,48},{48,64},{64,80},{80,96},{96,112},{112,128},... | collective-permute-start | bytes 3932168 | tf_op jit(solution)/shard_map/ppermute | solution.py:20
  93.0 20.6 %collective-permute-start.1 = (bf16[1,1,1024,640]{3,2,1,0:T(8,128)(2,1)}, bf16[1,1,1024,640]{3,2,1,0:T(8,128)(2,1)S(1)}, u32[]{:S(2)}, u32[]{:S(2)}) collective-permute-start(bf16[1,1,1024,640]{3,2,1,0:T(8,128)(2,1)} %fusion.12), channel_id=1, source_target_pairs={{16,0},{32,16},{48,32},{64,48},{80,64},{96,80},{112,96},{128,112},... | collective-permute-start | bytes 3932168 | tf_op jit(solution)/shard_map/ppermute | solution.py:21
  101.3 9.7 %copy-start.10 = (bf16[3,640,640]{1,2,0:T(8,128)(2,1)S(1)}, bf16[3,640,640]{1,2,0:T(8,128)(2,1)}, u32[]{:S(2)}) copy-start(bf16[3,640,640]{1,2,0:T(8,128)(2,1)} %all-gather.5.cloned.1.call-done) | copy-start | bytes 7372804
  124.8 7.0 %copy-start.13 = (f32[1,640]{1,0:T(1,128)S(1)}, f32[1,640]{1,0:T(1,128)}, u32[]{:S(2)}) copy-start(f32[1,640]{1,0:T(1,128)} %param.15) | copy-start | bytes 7684
  124.8 48.5 %all-to-all-start = ((bf16[16,128,640]{2,1,0:T(8,128)(2,1)}), bf16[16,128,640]{2,1,0:T(8,128)(2,1)}, u32[]{:S(2)}, u32[]{:S(2)}) async-start(bf16[16,128,640]{2,1,0:T(8,128)(2,1)} %reshape.221), calls=%async_computation | async-start | bytes 5242880 | tf_op jit(solution)/shard_map/all_to_all | solution.py:85
Sparse Core Ops, SparseCore 0:
  9.1 52.1 all-gather.2
  63.1 38.1 all-gather.4

commit v2 on v1

v2 whole, which is shorter than its diff:
```python
import jax
import jax.numpy as jnp
import numpy as np
from jax import lax
from jax.sharding import Mesh
from jax.sharding import PartitionSpec as P

GROUPS = 32
IMG_ROWS = 32
IMG_COLS = 32
PIX = 1024
CAP = 4
FSDP = ("z", "c")
BATCH = ("y", "x")


def with_halo(array, axis, dim):
    size, length = (lax.axis_size(axis), array.shape[dim])
    up = [(i, (i + 1) % size) for i in range(size - 1)]
    down = [(j, i) for i, j in up]
    last = lax.slice_in_dim(array, length - 1, length, axis=dim)
    leading = lax.slice_in_dim(array, 0, 1, axis=dim)
    before = lax.ppermute(last, axis, up)
    after = lax.ppermute(leading, axis, down)
    return jnp.concatenate([before, array, after], axis=dim)


def group_silu(values, gain):
    shape = values.shape
    width = shape[-1]
    grouped = values.astype(jnp.float32).reshape(-1, shape[-2], GROUPS, width // GROUPS)
    center = jnp.mean(grouped, axis=(1, 3), keepdims=True)
    spread = jnp.mean((grouped - center) ** 2, axis=(1, 3), keepdims=True)
    normed = ((grouped - center) * lax.rsqrt(spread + 1e-05)).reshape(shape) * gain
    return jax.nn.silu(normed).astype(jnp.bfloat16)


def gather_out_major(weights):
    turned = jnp.swapaxes(weights, 1, 2)
    return lax.all_gather(turned, FSDP, axis=1, tiled=True)


def nt_dot(a, b):
    return lax.dot_general(a, b, (((1,), (1,)), ((), ())), preferred_element_type=jnp.float32)


def per_device(
    latents, norm_gain, second_gain, spatial_w, temporal_w, critic_w, critic_head, targets, feasible
):
    cands = latents.shape[0]
    width = latents.shape[-1]
    hid = critic_w.shape[-1]

    core = lax.axis_index("c")
    half = hid // 2
    own_half = lax.dynamic_slice_in_dim(critic_w[0], core * half, half, axis=1)
    mine = lax.all_gather(own_half, BATCH, axis=0, tiled=False)
    other = lax.ppermute(mine, "c", [(0, 1), (1, 0)])
    heads = lax.all_gather(critic_head[0], BATCH, axis=0, tiled=False)
    heads_mine = lax.dynamic_slice_in_dim(heads, core * half, half, axis=1)
    heads_other = lax.dynamic_slice_in_dim(heads, (1 - core) * half, half, axis=1)

    spatial_full = gather_out_major(spatial_w)
    temporal_full = gather_out_major(temporal_w)

    first = group_silu(latents, norm_gain)
    padded = jnp.pad(
        first.reshape(cands, IMG_ROWS, IMG_COLS, width), ((0, 0), (1, 1), (1, 1), (0, 0))
    )
    total = jnp.zeros((cands * PIX, spatial_full.shape[1]), jnp.float32)
    for offset in range(9):
        row_off, col_off = divmod(offset, 3)
        window = padded[:, row_off : row_off + IMG_ROWS, col_off : col_off + IMG_COLS].reshape(
            -1, width
        )
        total = total + nt_dot(window, spatial_full[offset])
    section = (latents.astype(jnp.float32) + total.reshape(latents.shape)).astype(jnp.bfloat16)
    second = group_silu(section, second_gain)
    beside_all = with_halo(second, FSDP, 1)
    total = jnp.zeros((cands * PIX, temporal_full.shape[1]), jnp.float32)
    for tap in range(3):
        total = total + nt_dot(beside_all[:, tap].reshape(-1, width), temporal_full[tap])
    denoised = (section.astype(jnp.float32) + total.reshape(latents.shape)).astype(jnp.bfloat16)

    groups = mine.shape[0]
    slots = cands * CAP
    flat_targets = targets.reshape(-1)
    chosen = (flat_targets[:, None] == jnp.arange(groups, dtype=jnp.int32)[None, :]).astype(
        jnp.int32
    )
    earlier = jnp.cumsum(chosen, axis=0) - chosen
    slot_of = jnp.sum(earlier * chosen, axis=1)
    live = jnp.repeat(feasible.reshape(-1), IMG_ROWS) > 0
    position = flat_targets * slots + slot_of
    placing = (
        (jnp.arange(groups * slots, dtype=jnp.int32)[:, None] == position[None, :]) & live[None, :]
    ).astype(jnp.bfloat16)
    rows = denoised.reshape(cands * IMG_ROWS, IMG_COLS * width)
    block = (
        jnp.dot(placing, rows, preferred_element_type=jnp.float32)
        .astype(jnp.bfloat16)
        .reshape(groups, slots * IMG_COLS, width)
    )

    def slope_of(w, h):
        pre = jnp.einsum("gtc,gch->gth", block, w, preferred_element_type=jnp.float32)
        return ((1.0 - jnp.tanh(pre) ** 2) * h[:, None, :]).astype(jnp.bfloat16)

    grads = jnp.einsum(
        "gth,gch->gtc", slope_of(mine, heads_mine), mine, preferred_element_type=jnp.float32
    ) + jnp.einsum(
        "gth,gch->gtc", slope_of(other, heads_other), other, preferred_element_type=jnp.float32
    )
    returned = grads.astype(jnp.bfloat16).reshape(groups * slots, -1)
    back = jnp.dot(placing.T, returned, preferred_element_type=jnp.float32)
    guided = (rows.astype(jnp.float32) - back).astype(jnp.bfloat16)
    return guided.reshape(latents.shape)


def solution(mesh):
    fine = Mesh(np.asarray(mesh.devices).reshape(8, 2, 4, 4), ("z", "c", "y", "x"))
    in_specs = (
        P(BATCH, FSDP, None, None),
        P(),
        P(),
        P(None, None, FSDP),
        P(None, None, FSDP),
        P(BATCH, None, None),
        P(BATCH, None),
        P(BATCH, None, None),
        P(BATCH, FSDP),
    )
    out_specs = P(BATCH, FSDP, None, None)
    return jax.shard_map(
        per_device, mesh=fine, in_specs=in_specs, out_specs=out_specs, check_vma=False
    )
```

time: 235 us -> 254 us (1.081); the launches traced: 234 us -> 250 us
  waiting for transfers between devices: 97.8 us -> 124 us
  blocking collectives: 38.2 us -> 23.5 us
  matrix products: 46.2 us -> 60.6 us
  starting transfers between devices: 12.6 us -> 4.16 us
    all_gather x2 -> x3, waiting for transfers between devices: 48.2 us -> 113 us  [the longest x1 61.5 us: per_device(): mine = lax.all_gather(own_half, BATCH, axis=0, tiled=False)]
    all_to_all x1 -> x0, waiting for transfers between devices: 41.5 us -> none  [per_device(): arrived = lax.all_to_all(outgoing, 'batch', 0, 0, tiled=True)]
    all_to_all x1 -> x0, blocking collectives: 38.2 us -> none  [per_device(): lax.all_to_all(grads.reshape(groups, slots * IMG_COLS, width), 'batch', 0...]
    all_gather x0 -> x1, blocking collectives: none -> 23.5 us  [per_device(): heads = lax.all_gather(critic_head[0], BATCH, axis=0, tiled=False)]
    dot_general x14 -> x15, matrix products: 43.8 us -> 58.3 us  [the longest x12 34 us: nt_dot(): lax.dot_general(a, b, (((1,), (1,)), ((), ())), preferred_element_type=jn...]
    ppermute x1, waiting for transfers between devices: 0.01 us -> 9.37 us  [with_halo(): after = lax.ppermute(leading, axis, down)]
    all_to_all x1 -> x0, starting transfers between devices: 6.98 us -> none  [per_device(): arrived = lax.all_to_all(outgoing, 'batch', 0, 0, tiled=True)]
    ppermute x1, waiting for transfers between devices: 6.67 us -> 0.01 us  [with_halo(): before = lax.ppermute(last, axis, up)]
  transfers between devices with their start and end apart: 5 -> 6, of which waited for: 4 -> 3; matrix products, arithmetic and copies ran while one was open for 19% -> 24% of each run, Pallas kernels for 0% -> 0%
where the time goes in v2:
time: 254 us; the launch traced here: 250 us
  waiting for transfers between devices  124 us (49%)
  matrix products  60.6 us (24%)
  blocking collectives  23.5 us (9%)
  local copies, waits for them, and re-layouts  19.9 us (8%)
  between operations  14.2 us (6%)
  starting transfers between devices  4.16 us (2%)
  other arithmetic  3.74 us (1%)
    all_gather x1, waiting for transfers between devices, per_device(): mine = lax.all_gather(own_half, BATCH, axis=0, tiled=False)  61.5 us
    all_gather x2, waiting for transfers between devices, gather_out_major(): return lax.all_gather(turned, FSDP, axis=1, tiled=True)  51.4 us
    dot_general x12, matrix products, nt_dot(): lax.dot_general(a, b, (((1,), (1,)), ((), ())), preferred_element_type=jn...  34 us
    all_gather x1, blocking collectives, per_device(): heads = lax.all_gather(critic_head[0], BATCH, axis=0, tiled=False)  23.5 us
    dot_general x1, matrix products, per_device(): jnp.einsum('gth,gch->gtc', slope_of(other, heads_other), other, preferred...  11.3 us
    dot_general x1, matrix products, per_device(): jnp.einsum('gth,gch->gtc', slope_of(mine, heads_mine), mine, preferred_el...  10.6 us
    ppermute x1, waiting for transfers between devices, with_halo(): after = lax.ppermute(leading, axis, down)  9.37 us
    slice x1, local copies, waits for them, and re-layouts, per_device(): padded[:, row_off:row_off + IMG_ROWS, col_off:col_off + IMG_COLS]  5.28 us
  transfers between devices with their start and end apart: 6, of which 3 were waited for; matrix products, arithmetic and copies ran while one was open for 24% of the time, Pallas kernels for 0%

profile of v2, /device:TPU:64, one launch (start us, length us, event | category | flops | bytes accessed | tf_op | source)
XLA Modules:
  0.0 249.9 jit_solution(7458203786415808206)
XLA Ops:
  6.5 1.1 copy-done
  7.9 1.0 copy.15
  9.0 0.7 all-gather.5.cloned.1.call-update
  11.9 0.8 fusion.20
  12.7 5.3 %pad_slice_fusion = (bf16[1,32,32,640]{3,2,1,0:T(8,128)(2,1)}, bf16[1,32,32,640]{3,2,1,0:T(8,128)(2,1)}, bf16[1,32,32,640]{3,2,1,0:T(8,128)(2,1)}, bf16[1,32,32,...) fusion(bf16[1,32,32,640]{3,2,1,0:T(8,128)(2,1)S(1)} %bitcast.93), kind=kLoop, calls=%fused_computation.34 | loop fusion | bytes 11796480 | tf_op jit(solution)/shard_map/slice | solution.py:73
  18.0 61.5 %all-gather.9.cloned.1.call-done = bf16[16,640,320]{1,2,0:T(8,128)(2,1)} async-done(((bf16[1,640,320]{1,2,0:T(8,128)(2,1)}), bf16[16,640,320]{1,2,0:T(8,128)(2,1)}) %all-gather.9.cloned.1.call-update) | async-done | bytes 6553616 | tf_op jit(solution)/shard_map/all_gather | solution.py:57
  79.5 51.4 %all-gather.5.cloned.1.call-done = bf16[9,640,640]{2,1,0:T(8,128)(2,1)} async-done(((bf16[9,40,640]{2,1,0:T(8,128)(2,1)}), bf16[9,640,640]{2,1,0:T(8,128)(2,1)}) %all-gather.5.cloned.1.call-update) | async-done | bytes 7372816 | tf_op jit(solution)/shard_map/all_gather | solution.py:40
  131.0 2.6 %fusion.32 = f32[1024,640]{1,0:T(8,128)S(1)} fusion(bf16[1,1,1024,640]{3,2,1,0:T(8,128)(2,1)S(1)} %fusion.20, bf16[9,640,640]{2,1,0:T(8,128)(2,1)} %all-gather.5.cloned.1.call-done), kind=kOutput, calls=%fused_computation.49 | convolution fusion | flops 838860800 | bytes 4751360 | tf_op jit(solution)/shard_map/dot_general | solution.py:44
  133.6 2.6 %fusion.36 = f32[1024,640]{1,0:T(8,128)S(1)} fusion(bf16[1024,640]{1,0:T(8,128)(2,1)S(1)} %bitcast.101, bf16[9,640,640]{2,1,0:T(8,128)(2,1)} %all-gather.5.cloned.1.call-done), kind=kOutput, calls=%fused_computation.58 | convolution fusion | flops 838860800 | bytes 4751360 | tf_op jit(solution)/shard_map/dot_general | solution.py:44
  136.2 2.6 %fusion.37 = f32[1024,640]{1,0:T(8,128)S(1)} fusion(bf16[1024,640]{1,0:T(8,128)(2,1)S(1)} %bitcast.100, bf16[9,640,640]{2,1,0:T(8,128)(2,1)} %all-gather.5.cloned.1.call-done), kind=kOutput, calls=%fused_computation.60 | convolution fusion | flops 838860800 | bytes 4751360 | tf_op jit(solution)/shard_map/dot_general | solution.py:44
  138.8 2.6 %fusion.38 = f32[1024,640]{1,0:T(8,128)S(1)} fusion(bf16[1024,640]{1,0:T(8,128)(2,1)S(1)} %bitcast.99, bf16[9,640,640]{2,1,0:T(8,128)(2,1)} %all-gather.5.cloned.1.call-done), kind=kOutput, calls=%fused_computation.62 | convolution fusion | flops 838860800 | bytes 4751360 | tf_op jit(solution)/shard_map/dot_general | solution.py:44
  141.4 2.6 %fusion.39 = f32[1024,640]{1,0:T(8,128)S(1)} fusion(bf16[1024,640]{1,0:T(8,128)(2,1)S(1)} %bitcast.98, bf16[9,640,640]{2,1,0:T(8,128)(2,1)} %all-gather.5.cloned.1.call-done), kind=kOutput, calls=%fused_computation.65 | convolution fusion | flops 838860800 | bytes 4751360 | tf_op jit(solution)/shard_map/dot_general | solution.py:44
  144.0 2.6 %fusion.40 = f32[1024,640]{1,0:T(8,128)S(1)} fusion(bf16[1024,640]{1,0:T(8,128)(2,1)S(1)} %bitcast.97, bf16[9,640,640]{2,1,0:T(8,128)(2,1)} %all-gather.5.cloned.1.call-done), kind=kOutput, calls=%fused_computation.67 | convolution fusion | flops 838860800 | bytes 4751360 | tf_op jit(solution)/shard_map/dot_general | solution.py:44
  146.6 2.6 %fusion.41 = f32[1024,640]{1,0:T(8,128)S(1)} fusion(bf16[1024,640]{1,0:T(8,128)(2,1)S(1)} %bitcast.96, bf16[9,640,640]{2,1,0:T(8,128)(2,1)} %all-gather.5.cloned.1.call-done), kind=kOutput, calls=%fused_computation.69 | convolution fusion | flops 838860800 | bytes 4751360 | tf_op jit(solution)/shard_map/dot_general | solution.py:44
  149.2 4.1 %fusion.42 = f32[1024,640]{1,0:T(8,128)} fusion(bf16[1024,640]{1,0:T(8,128)(2,1)S(1)} %bitcast.95, bf16[9,640,640]{2,1,0:T(8,128)(2,1)} %all-gather.5.cloned.1.call-done), kind=kOutput, calls=%fused_computation.71 | convolution fusion | flops 838860800 | bytes 4751360 | tf_op jit(solution)/shard_map/dot_general | solution.py:44
  153.3 3.8 %convert_reduce_fusion = (f32[640]{0:T(1024)S(1)}, bf16[1,1,1024,640]{3,2,1,0:T(8,128)(2,1)S(1)}) fusion(bf16[1024,640]{1,0:T(8,128)(2,1)S(1)} %bitcast.94, bf16[9,640,640]{2,1,0:T(8,128)(2,1)} %all-gather.5.cloned.1.call-done, f32[1024,640]{1,0:T(8,128)S(1)} %fusion.36, f32[1024,640]{1,0:T(8,128)S(1)} %fusion.37, f32[1024,640]{1,0:T(8,128)S(1)} %fusion.38, ...), kind=kOutput, calls=%fused_computation.6 | convolution fusion | flops 847379840 | bytes 25725440 | tf_op jit(solution)/shard_map/dot_general | solution.py:44
  158.3 1.1 fusion.12
  159.4 2.2 collective-permute-start
  162.4 23.5 %all-gather = f32[16,1,640]{2,1,0:T(1,128)S(1)} all-gather(f32[1,1,640]{2,1,0:T(1,128)S(1)} %bitcast.104), channel_id=1, replica_groups=mesh['z'=8,'c'=2,'y'=4,'x'=4] {'y','x'}, dimensions={0}, use_global_device_ids=true | all-gather | bytes 43520 | tf_op jit(solution)/shard_map/all_gather | solution.py:59
  185.9 1.9 collective-permute-start.1
  188.2 2.6 %fusion.28 = f32[1024,640]{1,0:T(8,128)S(1)} fusion(bf16[1,1,1024,640]{3,2,1,0:T(8,128)(2,1)S(1)} %fusion.12, bf16[3,640,640]{2,1,0:T(8,128)(2,1)} %all-gather.7.cloned.1.call-done), kind=kOutput, calls=%fused_computation.45 | convolution fusion | flops 838860800 | bytes 4751360 | tf_op jit(solution)/shard_map/dot_general | solution.py:44
  190.9 2.7 %fusion.30 = f32[1024,640]{1,0:T(8,128)S(1)} fusion(bf16[1,1,1024,640]{3,2,1,0:T(8,128)(2,1)} %collective-permute-done, bf16[3,640,640]{2,1,0:T(8,128)(2,1)S(1)} %copy-done.13), kind=kOutput, calls=%fused_computation.47 | convolution fusion | flops 838860800 | bytes 4751360 | tf_op jit(solution)/shard_map/dot_general | solution.py:44
  193.5 9.4 %collective-permute-done.1 = bf16[1,1,1024,640]{3,2,1,0:T(8,128)(2,1)} collective-permute-done((bf16[1,1,1024,640]{3,2,1,0:T(8,128)(2,1)S(1)}, bf16[1,1,1024,640]{3,2,1,0:T(8,128)(2,1)}, u32[]{:S(2)}, u32[]{:S(2)}) %collective-permute-start.1) | collective-permute-done | bytes 1310752 | tf_op jit(solution)/shard_map/ppermute | solution.py:24
  202.9 2.8 %fusion.22 = bf16[1,1,1024,640]{3,2,1,0:T(8,128)(2,1)S(1)} fusion(bf16[1,1,1024,640]{3,2,1,0:T(8,128)(2,1)S(1)} %get-tuple-element.16, f32[1024,640]{1,0:T(8,128)S(1)} %fusion.30, f32[1024,640]{1,0:T(8,128)S(1)} %fusion.28, bf16[1,1,1024,640]{3,2,1,0:T(8,128)(2,1)} %collective-permute-done.1, bf16[3,640,640]{2,1,0:T(8,128)(2,1)S(1)} %copy-done.13), kind=kOutput, calls=%fused_computation.31 | convolution fusion | flops 842137600 | bytes 9994240 | tf_op jit(solution)/shard_map/dot_general | solution.py:44
  206.4 1.0 copy-done.3
  207.4 2.3 convolution_convert_fusion
  209.8 3.1 %reshape.219 = bf16[16,128,640]{2,1,0:T(8,128)(2,1)S(1)} reshape(bf16[64,20480]{1,0:T(8,128)(2,1)} %convolution_convert_fusion) | data formatting | bytes 5242880 | tf_op jit(solution)/shard_map/reshape | solution.py:102
  212.9 10.6 %fusion.23 = f32[16,128,640]{2,1,0:T(8,128)} fusion(bf16[16,640,320]{1,2,0:T(8,128)(2,1)} %all-gather.9.cloned.1.call-done, bf16[16,128,640]{2,1,0:T(8,128)(2,1)S(1)} %reshape.219, f32[16,320]{1,0:T(8,128)S(1)} %get-tuple-element.18), kind=kOutput, calls=%fused_computation.42 | convolution fusion | flops 1680343040 | bytes 14438400 | tf_op jit(solution)/shard_map/gth,gch->gtc/dot_general | solution.py:109
  223.5 11.3 %add_convert_fusion = bf16[16,128,640]{2,1,0:T(8,128)(2,1)} fusion(f32[16,128,640]{2,1,0:T(8,128)} %fusion.23, bf16[16,640,320]{1,2,0:T(8,128)(2,1)} %collective-permute-done.2, bf16[16,128,640]{2,1,0:T(8,128)(2,1)S(1)} %reshape.219, f32[16,320]{1,0:T(8,128)S(1)} %get-tuple-element.17), kind=kOutput, calls=%fused_computation.3 | convolution fusion | flops 1682964480 | bytes 17059840 | tf_op jit(solution)/shard_map/gth,gch->gtc/dot_general | solution.py:111
  234.9 4.6 %reshape.220 = bf16[64,20480]{1,0:T(8,128)(2,1)} reshape(bf16[16,128,640]{2,1,0:T(8,128)(2,1)} %add_convert_fusion) | data formatting | bytes 5242880 | tf_op jit(solution)/shard_map/reshape | solution.py:114
  239.5 2.4 fusion
  241.9 1.5 reshape.221
  (74 shorter events, 4.9 us)
Async XLA Ops:
  6.5 1.1 copy-start
  6.5 3.9 %copy-start.2 = (bf16[1,1,1024,640]{3,2,1,0:T(8,128)(2,1)S(1)}, bf16[1,1,1024,640]{3,2,1,0:T(8,128)(2,1)}, u32[]{:S(2)}) copy-start(bf16[1,1,1024,640]{3,2,1,0:T(8,128)(2,1)} %param.9) | copy-start | bytes 3932164
  6.5 73.0 %all-gather.9.cloned.1.call-start = ((), (), s32[]{:S(2)}) async-start(), calls=%async_computation.2 | async-start | bytes 6963200 | tf_op jit(solution)/shard_map/all_gather | solution.py:57
  7.7 4.2 %copy-start.14 = (f32[640]{0:T(1024)S(1)}, f32[640]{0:T(1024)}, u32[]{:S(2)}) copy-start(f32[640]{0:T(1024)} %param.10) | copy-start | bytes 7684
  8.9 122.0 %all-gather.5.cloned.1.call-start = ((), (), s32[]{:S(2)}) async-start(), calls=%async_computation | async-start | bytes 7833600 | tf_op jit(solution)/shard_map/all_gather | solution.py:40
  9.7 178.5 %all-gather.7.cloned.1.call-start = ((), (), s32[]{:S(2)}) async-start(), calls=%async_computation.1 | async-start | bytes 2611200 | tf_op jit(solution)/shard_map/all_gather | solution.py:40
  79.5 144.0 %collective-permute-start.2 = (bf16[16,640,320]{1,2,0:T(8,128)(2,1)}, bf16[16,640,320]{1,2,0:T(8,128)(2,1)}, u32[]{:S(2)}, u32[]{:S(2)}) collective-permute-start(bf16[16,640,320]{1,2,0:T(8,128)(2,1)} %all-gather.9.cloned.1.call-done), channel_id=1, source_target_pairs={{0,16},{16,0},{1,17},{17,1},{2,18},{18,2},{3,19},{19,3},{4,20},{20... | collective-permute-start | bytes 19660808 | tf_op jit(solution)/shard_map/ppermute | solution.py:58
  131.0 2.6 %copy-start.12 = (bf16[1,32,32,640]{3,2,1,0:T(8,128)(2,1)S(1)}, bf16[1,32,32,640]{3,2,1,0:T(8,128)(2,1)}, u32[]{:S(2)}) copy-start(bf16[1,32,32,640]{3,2,1,0:T(8,128)(2,1)} %get-tuple-element.11) | copy-start | bytes 3932164
  133.5 2.6 %copy-start.11 = (bf16[1,32,32,640]{3,2,1,0:T(8,128)(2,1)S(1)}, bf16[1,32,32,640]{3,2,1,0:T(8,128)(2,1)}, u32[]{:S(2)}) copy-start(bf16[1,32,32,640]{3,2,1,0:T(8,128)(2,1)} %get-tuple-element.10) | copy-start | bytes 3932164
  136.1 2.6 %copy-start.10 = (bf16[1,32,32,640]{3,2,1,0:T(8,128)(2,1)S(1)}, bf16[1,32,32,640]{3,2,1,0:T(8,128)(2,1)}, u32[]{:S(2)}) copy-start(bf16[1,32,32,640]{3,2,1,0:T(8,128)(2,1)} %get-tuple-element.9) | copy-start | bytes 3932164
  138.7 2.6 %copy-start.9 = (bf16[1,32,32,640]{3,2,1,0:T(8,128)(2,1)S(1)}, bf16[1,32,32,640]{3,2,1,0:T(8,128)(2,1)}, u32[]{:S(2)}) copy-start(bf16[1,32,32,640]{3,2,1,0:T(8,128)(2,1)} %get-tuple-element.8) | copy-start | bytes 3932164
  141.3 2.6 %copy-start.8 = (bf16[1,32,32,640]{3,2,1,0:T(8,128)(2,1)S(1)}, bf16[1,32,32,640]{3,2,1,0:T(8,128)(2,1)}, u32[]{:S(2)}) copy-start(bf16[1,32,32,640]{3,2,1,0:T(8,128)(2,1)} %get-tuple-element.7) | copy-start | bytes 3932164
  143.9 2.6 %copy-start.7 = (bf16[1,32,32,640]{3,2,1,0:T(8,128)(2,1)S(1)}, bf16[1,32,32,640]{3,2,1,0:T(8,128)(2,1)}, u32[]{:S(2)}) copy-start(bf16[1,32,32,640]{3,2,1,0:T(8,128)(2,1)} %get-tuple-element.6) | copy-start | bytes 3932164
  146.5 2.6 %copy-start.6 = (bf16[1,32,32,640]{3,2,1,0:T(8,128)(2,1)S(1)}, bf16[1,32,32,640]{3,2,1,0:T(8,128)(2,1)}, u32[]{:S(2)}) copy-start(bf16[1,32,32,640]{3,2,1,0:T(8,128)(2,1)} %get-tuple-element.12) | copy-start | bytes 3932164
  149.2 4.1 %copy-start.5 = (bf16[1,32,32,640]{3,2,1,0:T(8,128)(2,1)S(1)}, bf16[1,32,32,640]{3,2,1,0:T(8,128)(2,1)}, u32[]{:S(2)}) copy-start(bf16[1,32,32,640]{3,2,1,0:T(8,128)(2,1)} %get-tuple-element.5) | copy-start | bytes 3932164
  153.3 5.0 %copy-start.15 = (f32[640]{0:T(1024)S(1)}, f32[640]{0:T(1024)}, u32[]{:S(2)}) copy-start(f32[640]{0:T(1024)} %param.11) | copy-start | bytes 7684
  157.1 4.5 %copy-start.17 = (s32[1,32,1]{1,2,0:T(1,128)S(1)}, s32[1,32,1]{1,2,0:T(1,128)}, u32[]{:S(2)}) copy-start(s32[1,32,1]{1,2,0:T(1,128)} %param.16) | copy-start | bytes 388
  157.1 5.3 %copy-start.16 = (f32[1,640]{1,0:T(1,128)S(1)}, f32[1,640]{1,0:T(1,128)}, u32[]{:S(2)}) copy-start(f32[1,640]{1,0:T(1,128)} %param.15) | copy-start | bytes 7684
  159.4 31.5 %collective-permute-start = (bf16[1,1,1024,640]{3,2,1,0:T(8,128)(2,1)S(1)}, bf16[1,1,1024,640]{3,2,1,0:T(8,128)(2,1)}, u32[]{:S(2)}, u32[]{:S(2)}) collective-permute-start(bf16[1,1,1024,640]{3,2,1,0:T(8,128)(2,1)S(1)} %fusion.12), channel_id=1, source_target_pairs={{0,16},{16,32},{32,48},{48,64},{64,80},{80,96},{96,112},{112,128},... | collective-permute-start | bytes 3932168 | tf_op jit(solution)/shard_map/ppermute | solution.py:23
  185.9 17.0 %collective-permute-start.1 = (bf16[1,1,1024,640]{3,2,1,0:T(8,128)(2,1)S(1)}, bf16[1,1,1024,640]{3,2,1,0:T(8,128)(2,1)}, u32[]{:S(2)}, u32[]{:S(2)}) collective-permute-start(bf16[1,1,1024,640]{3,2,1,0:T(8,128)(2,1)S(1)} %fusion.12), channel_id=1, source_target_pairs={{16,0},{32,16},{48,32},{64,48},{80,64},{96,80},{112,96},{128,112},... | collective-permute-start | bytes 3932168 | tf_op jit(solution)/shard_map/ppermute | solution.py:24
  188.2 2.6 %copy-start.13 = (bf16[3,640,640]{2,1,0:T(8,128)(2,1)S(1)}, bf16[3,640,640]{2,1,0:T(8,128)(2,1)}, u32[]{:S(2)}) copy-start(bf16[3,640,640]{2,1,0:T(8,128)(2,1)} %all-gather.7.cloned.1.call-done) | copy-start | bytes 7372804
  206.4 1.1 copy-start.3
  234.9 4.6 %copy-start.4 = (bf16[32,20480]{1,0:T(8,128)(2,1)S(1)}, bf16[32,20480]{1,0:T(8,128)(2,1)}, u32[]{:S(2)}) copy-start(bf16[32,20480]{1,0:T(8,128)(2,1)} %copy-done.3) | copy-start | bytes 3932164
  239.5 3.9 %copy-start.1 = (bf16[1,640,640]{2,1,0:T(8,128)(2,1)S(1)}, bf16[1,640,640]{2,1,0:T(8,128)(2,1)}, u32[]{:S(2)}) copy-start(bf16[1,640,640]{2,1,0:T(8,128)(2,1)} %param.14) | copy-start | bytes 2457604
Sparse Core Ops, SparseCore 0:
  9.8 69.7 all-gather.8
  81.3 49.5 all-gather.4
  132.8 38.0 all-gather.6
